TPU v7x, 128 devices: a whole 4x4x4 slice. The times are simulated.
128 devices in a mesh: space: 32 (over x, z, core), feat: 4 (over y).
Axes of the slice: x: 4, y: 4, z: 4, core: 2. Of those that a mesh axis runs over, the one named last changes fastest.
Arguments:
- inputs: bfloat16 [2, 96, 180, 1024], P(None, 'space', None, 'feat'), may hold values from -15 to 15
- cotangent: bfloat16 [2, 96, 180, 1024], P(None, 'space', None, 'feat'), may hold values from -6 to 6
- spec_w1: float32 [2, 8, 128, 128], P(None, 'feat'), may hold values from -0.375 to 0.375
- spec_b1: float32 [2, 1024], P(None, 'feat'), may hold values from -0.3 to 0.3
- spec_w2: float32 [2, 8, 128, 128], P(None, 'feat'), may hold values from -0.375 to 0.375
- spec_b2: float32 [2, 1024], P(None, 'feat'), may hold values from -0.3 to 0.3
- up_weight: bfloat16 [1024, 4096], P(None, 'feat'), may hold values from -0.1875 to 0.1875
- down_weight: bfloat16 [4096, 1024], P('feat'), may hold values from -0.09375 to 0.09375
Outputs:
- output: bfloat16 [2, 96, 180, 1024], P(None, 'space', None, 'feat')
- grad_input: bfloat16 [2, 96, 180, 1024], P(None, 'space', None, 'feat')
All inputs are finite; a program needn't handle non-finite values.
Results may differ from a plain program's by a relative error of at most 0.0102.
Values may be sent and summed in bfloat16 or wider, within the bound.
No kernel may reach another device: no remote copies, remote signals or barrier semaphores. Data moves between devices by JAX's collectives and lax.ppermute only.
A program may use at most 128 MiB of HBM per device.

v0:
```python
import math
import jax
import jax.numpy as jnp
from jax import lax
from jax.sharding import PartitionSpec as P

EPSILON = 1e-05
SHRINK_LEVEL = 0.1
HIGHEST = lax.Precision.HIGHEST


def longitude_tables(width_lon):
    mode_count = width_lon // 2 + 1
    cell_index = jnp.arange(width_lon, dtype=jnp.int32)[:, None]
    wave_number = jnp.arange(mode_count, dtype=jnp.int32)[None, :]
    phase_angle = (
        2.0 * math.pi / width_lon * (cell_index * wave_number % width_lon).astype(jnp.float32)
    )
    scaling = 1.0 / math.sqrt(width_lon)
    cos_fwd = jnp.cos(phase_angle) * scaling
    sin_fwd = -jnp.sin(phase_angle) * scaling
    doubled = jnp.where((wave_number == 0) | (wave_number * 2 == width_lon), 1.0, 2.0).astype(
        jnp.float32
    )
    return (cos_fwd, sin_fwd, cos_fwd * doubled, sin_fwd * doubled)


def padded_tables(width_lon, multiple):
    tables = longitude_tables(width_lon)
    modes = tables[0].shape[1]
    extra = -modes % multiple
    return tuple((jnp.pad(table, ((0, 0), (0, extra))) for table in tables))


def lat_apply(table, field):
    return jnp.einsum("gh,bhkc->bgkc", table, field, precision=HIGHEST)


def complex_latitude(table_cos, table_sin, real_part, imag_part, inverse):
    if inverse:
        return (
            lat_apply(table_cos, real_part) + lat_apply(table_sin, imag_part),
            lat_apply(table_cos, imag_part) - lat_apply(table_sin, real_part),
        )
    return (
        lat_apply(table_cos, real_part) - lat_apply(table_sin, imag_part),
        lat_apply(table_cos, imag_part) + lat_apply(table_sin, real_part),
    )


def lon_forward(field, table):
    return jnp.einsum("brwc,wk->brkc", field, table, precision=HIGHEST)


def lon_back(spec, table):
    return jnp.einsum("brkc,wk->brwc", spec, table, precision=HIGHEST)


def to_blocks(field, block_size):
    return field.reshape(field.shape[:-1] + (field.shape[-1] // block_size, block_size))


def block_mult(field, weights):
    return jnp.einsum("...nc,nce->...ne", field, weights, precision=HIGHEST)


def block_mult_back(field, weights):
    return jnp.einsum("...ne,nce->...nc", field, weights, precision=HIGHEST)


def block_product(real_part, imag_part, weights):
    return (
        block_mult(real_part, weights[0]) - block_mult(imag_part, weights[1]),
        block_mult(real_part, weights[1]) + block_mult(imag_part, weights[0]),
    )


def block_adjoint(real_part, imag_part, weights):
    return (
        block_mult_back(real_part, weights[0]) + block_mult_back(imag_part, weights[1]),
        block_mult_back(imag_part, weights[0]) - block_mult_back(real_part, weights[1]),
    )


def latitude_tables(length):
    index_row = jnp.arange(length, dtype=jnp.int32)
    phase_angle = (
        2.0
        * math.pi
        / length
        * (index_row[:, None] * index_row[None, :] % length).astype(jnp.float32)
    )
    scaling = 1.0 / math.sqrt(length)
    return (jnp.cos(phase_angle) * scaling, -jnp.sin(phase_angle) * scaling)


def to_columns(real_part, imag_part, link_type):
    stacked = jnp.stack([real_part, imag_part]).astype(link_type)
    moved = lax.all_to_all(stacked, "space", 3, 2, tiled=True).astype(jnp.float32)
    return (moved[0], moved[1])


def to_rows(real_part, imag_part, link_type):
    stacked = jnp.stack([real_part, imag_part]).astype(link_type)
    moved = lax.all_to_all(stacked, "space", 2, 3, tiled=True).astype(jnp.float32)
    return (moved[0], moved[1])


def enter_spectrum(real_part, imag_part, tables_lat, link_type=jnp.float32):
    table_cos, table_sin = tables_lat
    real_part, imag_part = to_columns(real_part, imag_part, link_type)
    return complex_latitude(table_cos, table_sin, real_part, imag_part, False)


def leave_spectrum(real_part, imag_part, tables_lat, link_type=jnp.float32):
    table_cos, table_sin = tables_lat
    real_part, imag_part = complex_latitude(table_cos, table_sin, real_part, imag_part, True)
    return to_rows(real_part, imag_part, link_type)


def complex_operator(real_block, imag_block):
    return jnp.stack([jnp.stack([real_block, -imag_block]), jnp.stack([imag_block, real_block])])


def lat_stacked(operator, field, precision=lax.Precision.HIGH):
    return jnp.einsum("pqkh,qbhlc->pbklc", operator, field, precision=precision)


def lon_stacked_forward(field, tables, precision=lax.Precision.HIGH):
    return jnp.einsum("brwc,pwk->pbrkc", field, tables, precision=precision)


def lon_stacked_back(spec, tables, precision=lax.Precision.HIGH):
    return jnp.einsum("pbrkc,pwk->brwc", spec, tables, precision=precision)


def block_operator(weights):
    return jnp.moveaxis(complex_operator(weights[0], weights[1]), 2, 0)


def block_stacked(field, operator):
    return jnp.einsum("qbklnc,npqce->pbklne", field, operator, precision=lax.Precision.HIGH)


def block_stacked_adjoint(field, operator):
    return jnp.einsum("pbklne,npqce->qbklnc", field, operator, precision=lax.Precision.DEFAULT)


def stacked_columns(field, link_type):
    return lax.all_to_all(field.astype(link_type), "space", 3, 2, tiled=True).astype(jnp.float32)


def stacked_rows(field, link_type):
    return lax.all_to_all(field.astype(link_type), "space", 2, 3, tiled=True).astype(jnp.float32)


def token_sums(first_term, second_term):
    pair = jnp.stack([first_term, second_term])
    count = lax.axis_size("feat")
    shifted = jnp.stack(
        [pair]
        + [
            lax.ppermute(pair, "feat", [(i, (i + count - shift) % count) for i in range(count)])
            for shift in range(1, count)
        ]
    )
    total = shifted[0]
    for source in range(1, count):
        total = total + shifted[source]
    return (total[0], total[1])


def ring_send(block):
    count = lax.axis_size("feat")
    return [block] + [
        lax.ppermute(block, "feat", [(i, (i + shift) % count) for i in range(count)])
        for shift in range(1, count)
    ]


def ring_assemble(parts):
    count = len(parts)
    position = lax.axis_index("feat")
    block = parts[0]
    width = block.shape[-1]
    whole = jnp.zeros(block.shape[:-1] + (width * count,), block.dtype)
    for shift, moved in enumerate(parts):
        source = (position + count - shift) % count
        whole = lax.dynamic_update_slice_in_dim(whole, moved, source * width, axis=block.ndim - 1)
    return whole


def channel_share(term):
    return lax.psum_scatter(
        term.astype(jnp.bfloat16), "feat", scatter_dimension=3, tiled=True
    ).astype(jnp.float32)


def gelu_value(field):
    return 0.5 * field * (1.0 + lax.erf(field * (1.0 / math.sqrt(2.0))))


def gelu_slope(field):
    return 0.5 * (1.0 + lax.erf(field * (1.0 / math.sqrt(2.0)))) + field * jnp.exp(
        -0.5 * field * field
    ) * (1.0 / math.sqrt(2.0 * math.pi))


def per_device(inputs, cotangent, spec_w1, spec_b1, spec_w2, spec_b2, up_weight, down_weight):
    full_width = up_weight.shape[0]
    block_size = spec_w1.shape[2]
    tables_lon = padded_tables(inputs.shape[2], lax.axis_size("space"))
    tables_lat = latitude_tables(inputs.shape[1] * lax.axis_size("space"))
    cos_fwd, sin_fwd, cos_inv, sin_inv = tables_lon
    table_cos, table_sin = tables_lat
    operators = (
        jnp.stack([cos_fwd, sin_fwd]),
        jnp.stack([cos_inv, sin_inv]),
        complex_operator(table_cos, table_sin),
        complex_operator(table_cos, -table_sin),
        block_operator(spec_w1),
        block_operator(spec_w2),
    )
    operators = lax.optimization_barrier(operators)
    lon_fwd_tables, lon_inv_tables, lat_forward_op, lat_inverse_op, first_op, second_op = operators
    values = inputs.astype(jnp.float32)
    cotangent_parts = lax.all_gather(cotangent, "feat", axis=3, tiled=True)
    first_sum, second_sum = token_sums(jnp.sum(values, axis=-1), jnp.sum(values * values, axis=-1))
    mean_one = first_sum[..., None] / full_width
    rstd_one = lax.rsqrt(second_sum[..., None] / full_width - mean_one * mean_one + EPSILON)
    normed = (values - mean_one) * rstd_one
    spec = lat_stacked(
        lat_forward_op, stacked_columns(lon_stacked_forward(normed, lon_fwd_tables), jnp.float32)
    )
    spec_blocks = to_blocks(spec, block_size)
    bias_one = to_blocks(spec_b1, block_size)[:, None, None, None]
    bias_two = to_blocks(spec_b2, block_size)[:, None, None, None]
    first = jax.nn.relu(block_stacked(spec_blocks, first_op) + bias_one)
    second = block_stacked(first, second_op) + bias_two
    shrunk = (second - jnp.clip(second, -SHRINK_LEVEL, SHRINK_LEVEL)).reshape(spec.shape)
    shrunk, cotangent_parts = lax.optimization_barrier((shrunk, cotangent_parts))
    whole_cotangent = cotangent_parts
    filtered = lon_stacked_back(
        stacked_rows(lat_stacked(lat_inverse_op, shrunk, lax.Precision.DEFAULT), jnp.bfloat16),
        lon_inv_tables,
        lax.Precision.DEFAULT,
    )
    residual = (filtered + normed + values).astype(jnp.bfloat16)
    residual_vals = residual.astype(jnp.float32)
    whole_residual = lax.all_gather(residual, "feat", axis=3, tiled=True)
    grad_act = jnp.einsum(
        "brwd,hd->brwh", whole_cotangent, down_weight, preferred_element_type=jnp.float32
    )
    whole_residual, grad_act = lax.optimization_barrier((whole_residual, grad_act))
    whole_vals = whole_residual.astype(jnp.float32)
    mean_two = jnp.sum(whole_vals, axis=-1, keepdims=True) / full_width
    square_two = jnp.sum(whole_vals * whole_vals, axis=-1, keepdims=True) / full_width
    rstd_two = lax.rsqrt(square_two - mean_two * mean_two + EPSILON)
    vhat = (whole_vals - mean_two) * rstd_two
    hidden = jnp.einsum(
        "brwd,dh->brwh", vhat.astype(jnp.bfloat16), up_weight, preferred_element_type=jnp.float32
    )
    activated = gelu_value(hidden).astype(jnp.bfloat16)
    mixed_term = jnp.einsum(
        "brwh,hd->brwd", activated, down_weight, preferred_element_type=jnp.float32
    )
    output = (residual_vals + channel_share(mixed_term)).astype(jnp.bfloat16)
    grad_hidden = (grad_act * gelu_slope(hidden)).astype(jnp.bfloat16)
    grad_term = jnp.einsum(
        "brwh,dh->brwd", grad_hidden, up_weight, preferred_element_type=jnp.float32
    )
    total_one, total_two = token_sums(
        jnp.sum(grad_term, axis=-1), jnp.sum(grad_term * vhat, axis=-1)
    )
    grad_vhat = channel_share(grad_term)
    own_hat = (residual_vals - mean_two) * rstd_two
    grad_residual = cotangent.astype(jnp.float32) + rstd_two * (
        grad_vhat
        - total_one[..., None] / full_width
        - own_hat * (total_two[..., None] / full_width)
    )
    grad_spec = lat_stacked(
        lat_forward_op,
        stacked_columns(
            lon_stacked_forward(grad_residual, lon_inv_tables, lax.Precision.DEFAULT), jnp.bfloat16
        ),
        lax.Precision.DEFAULT,
    )
    grad_second = jnp.where(jnp.abs(second) > SHRINK_LEVEL, to_blocks(grad_spec, block_size), 0.0)
    grad_first = jnp.where(first > 0.0, block_stacked_adjoint(grad_second, second_op), 0.0)
    grad_spectrum = block_stacked_adjoint(grad_first, first_op).reshape(spec.shape)
    grad_normed = grad_residual + lon_stacked_back(
        stacked_rows(
            lat_stacked(lat_inverse_op, grad_spectrum, lax.Precision.DEFAULT), jnp.bfloat16
        ),
        lon_fwd_tables,
        lax.Precision.DEFAULT,
    )
    norm_one, norm_two = token_sums(
        jnp.sum(grad_normed, axis=-1), jnp.sum(grad_normed * normed, axis=-1)
    )
    grad_input = grad_residual + rstd_one * (
        grad_normed - norm_one[..., None] / full_width - normed * (norm_two[..., None] / full_width)
    )
    return (output, grad_input.astype(jnp.bfloat16))


def solution(mesh):
    return jax.shard_map(
        per_device,
        mesh=mesh,
        in_specs=(
            P(None, "space", None, "feat"),
            P(None, "space", None, "feat"),
            P(None, "feat", None, None),
            P(None, "feat"),
            P(None, "feat", None, None),
            P(None, "feat"),
            P(None, "feat"),
            P("feat", None),
        ),
        out_specs=(P(None, "space", None, "feat"), P(None, "space", None, "feat")),
        check_vma=False,
    )
```

profile of v0, /device:TPU:1, one launch (start us, length us, event | category | flops | bytes accessed | tf_op | source)
XLA Modules:
  0.0 219.6 jit_solution(13806531281613694137)
XLA Ops:
  7.2 1.7 convert_reduce_fusion.1
  9.0 3.8 %collective-permute-start.1 = (f32[2,2,3,180]{3,2,1,0:T(4,128)S(1)}, f32[2,2,3,180]{3,2,1,0:T(4,128)S(1)}, u32[]{:S(2)}, u32[]{:S(2)}) collective-permute-start(f32[2,2,3,180]{3,2,1,0:T(4,128)S(1)} %pad_maximum_fusion.8), channel_id=1, source_target_pairs={{0,2},{1,3},{2,0},{3,1},{4,6},{5,7},{6,4},{7,5},{8,10},{9,11},{10,... | collective-permute-start | bytes 25928 | tf_op jit(solution)/shard_map/ppermute | solution.py:163
  13.2 2.3 %collective-permute-start = (f32[2,2,3,180]{3,2,1,0:T(4,128)S(1)}, f32[2,2,3,180]{3,2,1,0:T(4,128)S(1)}, u32[]{:S(2)}, u32[]{:S(2)}) collective-permute-start(f32[2,2,3,180]{3,2,1,0:T(4,128)S(1)} %pad_maximum_fusion.8), channel_id=1, source_target_pairs={{0,3},{1,0},{2,1},{3,2},{4,7},{5,4},{6,5},{7,6},{8,11},{9,8},{10,9... | collective-permute-start | bytes 25928 | tf_op jit(solution)/shard_map/ppermute | solution.py:163
  18.2 1.1 maximum_bitcast_fusion.1
  22.0 28.2 %all_to_all.72 = f32[2,2,3,96,256]{4,1,2,0,3:T(2,128)S(1)} all-to-all(f32[2,2,3,96,256]{4,1,2,0,3:T(2,128)S(1)} %copy.96), channel_id=1, replica_groups=mesh['space'=32,'feat'=4] {'space'}, dimensions={3} | all-to-all | bytes 2359296 | tf_op jit(solution)/shard_map/all_to_all | solution.py:150
  51.3 1.6 reshape.195
  52.9 2.1 fusion.31
  57.7 1.4 fusion.42
  59.8 16.0 %all_to_all.73 = bf16[2,2,96,3,256]{4,0,3,1,2:T(2,128)(2,1)S(1)} all-to-all(bf16[2,2,96,3,256]{4,0,3,1,2:T(2,128)(2,1)S(1)} %copy.108), channel_id=1, replica_groups=mesh['space'=32,'feat'=4] {'space'}, dimensions={2} | all-to-all | bytes 1179648 | tf_op jit(solution)/shard_map/all_to_all | solution.py:154
  76.2 1.3 fusion.37
  77.6 6.9 %fusion.16 = f32[2,3,180,1024]{3,2,1,0:T(8,128)} fusion(bf16[2,3,180,1024]{3,0,2,1:T(2,128)(2,1)} %all-gather.3.cloned.1.call-done, bf16[1024,1024]{1,0:T(8,128)(2,1)} %param.15), kind=kOutput, calls=%fused_computation.20 | convolution fusion | flops 2264924160 | bytes 8732672 | tf_op jit(solution)/shard_map/brwd,hd->brwh/dot_general | solution.py:251
  84.5 23.0 %all-gather.5.cloned.1.call-done = bf16[2,3,180,1024]{3,2,1,0:T(8,128)(2,1)} async-done(((bf16[2,3,180,256]{3,2,1,0:T(8,128)(2,1)}), bf16[2,3,180,1024]{3,2,1,0:T(8,128)(2,1)}) %all-gather.5.cloned.1.call-update) | async-done | bytes 2211856 | tf_op jit(solution)/shard_map/all_gather | solution.py:250
  107.6 2.5 %convert_reduce_fusion = (f32[2,3,180]{2,1,0:T(4,128)S(1)}, f32[2,3,180]{2,1,0:T(4,128)S(1)}) fusion(bf16[2,3,180,1024]{3,2,1,0:T(8,128)(2,1)} %all-gather.5.cloned.1.call-done), kind=kLoop, calls=%fused_computation.3 | loop fusion | flops 4421520 | bytes 2220480 | tf_op jit(solution)/shard_map/reduce_sum | solution.py:256
  110.2 2.8 %fusion.14 = f32[2,3,180,1024]{3,2,1,0:T(8,128)S(1)} fusion(bf16[2,3,180,1024]{3,2,1,0:T(8,128)(2,1)S(1)} %copy-done.8, f32[2,3,180]{2,1,0:T(4,128)S(1)} %get-tuple-element.60, f32[2,3,180]{2,1,0:T(4,128)S(1)} %get-tuple-element.59, bf16[1024,1024]{1,0:T(8,128)(2,1)S(1)} %copy-done), kind=kOutput, calls=%fused_computation.19 | convolution fusion | flops 2269347840 | bytes 8741312 | tf_op jit(solution)/shard_map/brwd,dh->brwh/dot_general | solution.py:260
  113.1 5.4 %fusion.123 = (f32[2,3,180]{2,1,0:T(4,128)S(1)}, f32[2,3,180]{2,1,0:T(4,128)S(1)}, bf16[2,3,180,1024]{3,2,1,0:T(8,128)(2,1)}) fusion(f32[2,3,180]{2,1,0:T(4,128)S(1)} %get-tuple-element.60, f32[2,3,180]{2,1,0:T(4,128)S(1)} %get-tuple-element.59, bf16[2,3,180,1024]{3,2,1,0:T(8,128)(2,1)S(1)} %copy-done.8, bf16[1024,1024]{1,0:T(8,128)(2,1)S(1)} %copy-done, ...), kind=kOutput, calls=%fused_computation.189 | convolution fusion | flops 2283722752 | bytes 15385472 | tf_op jit(solution)/shard_map/brwh,dh->brwd/dot_general | solution.py:269
  118.5 6.9 %fusion.28 = bf16[2,3,180,1024]{3,2,1,0:T(8,128)(2,1)} fusion(bf16[1024,1024]{1,0:T(8,128)(2,1)} %param.15, f32[2,3,180,1024]{3,2,1,0:T(8,128)} %copy-done.19), kind=kOutput, calls=%fused_computation.36 | convolution fusion | flops 2271559680 | bytes 8732672 | tf_op jit(solution)/shard_map/brwh,hd->brwd/dot_general | solution.py:264
  125.5 2.5 %collective-permute-start.4 = (f32[2,2,3,180]{3,2,1,0:T(4,128)S(1)}, f32[2,2,3,180]{3,2,1,0:T(4,128)S(1)}, u32[]{:S(2)}, u32[]{:S(2)}) collective-permute-start(f32[2,2,3,180]{3,2,1,0:T(4,128)S(1)} %pad_maximum_fusion.9), channel_id=1, source_target_pairs={{0,2},{1,3},{2,0},{3,1},{4,6},{5,7},{6,4},{7,5},{8,10},{9,11},{10,... | collective-permute-start | bytes 25928 | tf_op jit(solution)/shard_map/ppermute | solution.py:163
  128.0 2.7 %collective-permute-start.3 = (f32[2,2,3,180]{3,2,1,0:T(4,128)S(1)}, f32[2,2,3,180]{3,2,1,0:T(4,128)S(1)}, u32[]{:S(2)}, u32[]{:S(2)}) collective-permute-start(f32[2,2,3,180]{3,2,1,0:T(4,128)S(1)} %pad_maximum_fusion.9), channel_id=1, source_target_pairs={{0,3},{1,0},{2,1},{3,2},{4,7},{5,4},{6,5},{7,6},{8,11},{9,8},{10,9... | collective-permute-start | bytes 25928 | tf_op jit(solution)/shard_map/ppermute | solution.py:163
  130.7 1.3 collective-permute-done.5
  132.0 19.8 %reduce-scatter.5.cloned.1.call-done = bf16[2,3,180,256]{3,2,1,0:T(8,128)(2,1)} async-done(((bf16[2,3,180,1024]{3,2,1,0:T(8,128)(2,1)}), bf16[2,3,180,256]{3,2,1,0:T(8,128)(2,1)}) %reduce-scatter.5.cloned.1.call-update) | async-done | bytes 552976 | tf_op jit(solution)/shard_map/reduce_scatter | solution.py:194
  151.8 2.3 %fusion.40 = bf16[2,2,3,96,256]{4,3,2,1,0:T(8,128)(2,1)S(1)} fusion(bf16[2,180,96]{2,1,0:T(8,128)(2,1)} %pad_maximum_fusion.3, bf16[2,3,180,256]{3,2,1,0:T(8,128)(2,1)} %fusion.37, bf16[2,3,180,256]{3,2,1,0:T(8,128)(2,1)} %reduce-scatter.5.cloned.1.call-done, bf16[2,3,180,256]{3,0,2,1:T(2,128)(2,1)} %param.9, f32[2,3,180]{2,1,0:T(4,128)S(1)} %get-tuple-element.58, ...), kind=kOutput, calls=%fused_computation.61 | convolution fusion | flops 108933120 | bytes 2335104 | tf_op jit(solution)/shard_map/brwc,pwk->pbrkc/dot_general | solution.py:130
  154.7 19.7 %all_to_all.74 = bf16[2,2,3,96,256]{4,1,2,0,3:T(2,128)(2,1)S(1)} all-to-all(bf16[2,2,3,96,256]{4,1,2,0,3:T(2,128)(2,1)S(1)} %copy.114), channel_id=1, replica_groups=mesh['space'=32,'feat'=4] {'space'}, dimensions={3} | all-to-all | bytes 1179648 | tf_op jit(solution)/shard_map/all_to_all | solution.py:150
  174.8 1.2 convolution_bitcast_fusion.8
  176.0 2.5 %reshape.229 = bf16[2,2,96,3,2,128]{5,4,2,0,3,1:T(2,128)(2,1)} reshape(bf16[2,2,96,3,256]{4,2,0,3,1:T(8,128)(2,1)} %convolution_bitcast_fusion.8) | data formatting | bytes 1179648 | tf_op jit(solution)/shard_map/reshape | solution.py:60
  178.5 2.1 fusion.39
  183.0 15.9 %all_to_all.75 = bf16[2,2,96,3,256]{4,0,3,1,2:T(2,128)(2,1)S(1)} all-to-all(bf16[2,2,96,3,256]{4,0,3,1,2:T(2,128)(2,1)S(1)} %copy.126), channel_id=1, replica_groups=mesh['space'=32,'feat'=4] {'space'}, dimensions={2} | all-to-all | bytes 1179648 | tf_op jit(solution)/shard_map/all_to_all | solution.py:154
  199.4 2.7 %fusion.124 = (f32[2,3,180]{2,1,0:T(4,128)S(1)}, f32[2,3,180]{2,1,0:T(4,128)S(1)}, f32[2,3,180,256]{3,2,1,0:T(8,128)}) fusion(f32[2,3,180]{2,1,0:T(4,128)S(1)} %fusion.115, f32[2,3,180]{2,1,0:T(4,128)S(1)} %fusion.116, bf16[2,3,180,256]{3,0,2,1:T(2,128)(2,1)S(1)} %copy-done.4, bf16[2,2,3,96,256]{4,1,3,2,0:T(2,128)(2,1)S(1)} %bitcast.284, ...), kind=kOutput, calls=%fused_computation.190 | convolution fusion | flops 110866320 | bytes 4080384 | tf_op jit(solution)/shard_map/pbrkc,pwk->brwc/dot_general | solution.py:134
  202.1 1.3 collective-permute-start.7
  203.4 2.6 %collective-permute-start.6 = (f32[2,2,3,180]{3,2,1,0:T(4,128)S(1)}, f32[2,2,3,180]{3,2,1,0:T(4,128)S(1)}, u32[]{:S(2)}, u32[]{:S(2)}) collective-permute-start(f32[2,2,3,180]{3,2,1,0:T(4,128)S(1)} %pad_maximum_fusion.10), channel_id=1, source_target_pairs={{0,3},{1,0},{2,1},{3,2},{4,7},{5,4},{6,5},{7,6},{8,11},{9,8},{10,9... | collective-permute-start | bytes 25928 | tf_op jit(solution)/shard_map/ppermute | solution.py:163
  207.3 3.4 %fusion.68 = (bf16[2,3,180,256]{3,2,1,0:T(8,128)(2,1)S(1)}, bf16[2,3,180,256]{3,2,1,0:T(8,128)(2,1)S(1)}) fusion(f32[2,3,180,256]{3,2,1,0:T(8,128)} %get-tuple-element.64, f32[2,3,180]{2,1,0:T(4,128)S(1)} %get-tuple-element.56, f32[2,3,180]{2,1,0:T(4,128)S(1)} %get-tuple-element.55, f32[2,3,180]{2,1,0:T(4,128)S(1)} %fusion.115, ...), kind=kLoop, calls=%fused_computation.92 | loop fusion | flops 6082560 | bytes 5011200 | tf_op jit(solution)/shard_map/convert_element_type | solution.py:305
  210.6 1.2 copy.131
  211.9 1.2 copy.130
  (111 shorter events, 15.7 us)
Async XLA Ops:
  7.2 103.0 %copy-start = (bf16[1024,1024]{1,0:T(8,128)(2,1)S(1)}, bf16[1024,1024]{1,0:T(8,128)(2,1)}, u32[]{:S(2)}) copy-start(bf16[1024,1024]{1,0:T(8,128)(2,1)} %param.14) | copy-start | bytes 6291460
  7.2 10.1 %copy-start.14 = (f32[2,2,128,128]{3,2,1,0:T(8,128)S(1)}, f32[2,2,128,128]{3,2,1,0:T(8,128)}, u32[]{:S(2)}) copy-start(f32[2,2,128,128]{3,2,1,0:T(8,128)} %param.10) | copy-start | bytes 786436
  7.2 50.5 %all-gather.3.cloned.1.call-start = ((), (), s32[]{:S(2)}) async-start(), calls=%async_computation.6 | async-start | bytes 2764800 | tf_op jit(solution)/shard_map/all_gather | solution.py:227
  9.0 8.4 %copy-start.15 = (f32[2,2,128,128]{3,2,1,0:T(8,128)S(1)}, f32[2,2,128,128]{3,2,1,0:T(8,128)}, u32[]{:S(2)}) copy-start(f32[2,2,128,128]{3,2,1,0:T(8,128)} %param.12) | copy-start | bytes 786436
  9.0 11.0 %collective-permute-start.1 = (f32[2,2,3,180]{3,2,1,0:T(4,128)S(1)}, f32[2,2,3,180]{3,2,1,0:T(4,128)S(1)}, u32[]{:S(2)}, u32[]{:S(2)}) collective-permute-start(f32[2,2,3,180]{3,2,1,0:T(4,128)S(1)} %pad_maximum_fusion.8), channel_id=1, source_target_pairs={{0,2},{1,3},{2,0},{3,1},{4,6},{5,7},{6,4},{7,5},{8,10},{9,11},{10,... | collective-permute-start | bytes 25928 | tf_op jit(solution)/shard_map/ppermute | solution.py:163
  12.8 7.2 %collective-permute-start.2 = (f32[2,2,3,180]{3,2,1,0:T(4,128)S(1)}, f32[2,2,3,180]{3,2,1,0:T(4,128)S(1)}, u32[]{:S(2)}, u32[]{:S(2)}) collective-permute-start(f32[2,2,3,180]{3,2,1,0:T(4,128)S(1)} %pad_maximum_fusion.8), channel_id=1, source_target_pairs={{0,1},{1,2},{2,3},{3,0},{4,5},{5,6},{6,7},{7,4},{8,9},{9,10},{10,1... | collective-permute-start | bytes 25928 | tf_op jit(solution)/shard_map/ppermute | solution.py:163
  13.2 6.8 %collective-permute-start = (f32[2,2,3,180]{3,2,1,0:T(4,128)S(1)}, f32[2,2,3,180]{3,2,1,0:T(4,128)S(1)}, u32[]{:S(2)}, u32[]{:S(2)}) collective-permute-start(f32[2,2,3,180]{3,2,1,0:T(4,128)S(1)} %pad_maximum_fusion.8), channel_id=1, source_target_pairs={{0,3},{1,0},{2,1},{3,2},{4,7},{5,4},{6,5},{7,6},{8,11},{9,8},{10,9... | collective-permute-start | bytes 25928 | tf_op jit(solution)/shard_map/ppermute | solution.py:163
  15.5 92.1 %all-gather.5.cloned.1.call-start = ((), (), s32[]{:S(2)}) async-start(), calls=%async_computation.7 | async-start | bytes 2826240 | tf_op jit(solution)/shard_map/all_gather | solution.py:250
  17.4 2.6 %copy-start.11 = (f32[2,180,96]{2,1,0:T(8,128)}, f32[2,180,96]{2,1,0:T(8,128)S(1)}, u32[]{:S(2)}) copy-start(f32[2,180,96]{2,1,0:T(8,128)S(1)} %pad_maximum_fusion.2) | copy-start | bytes 414724
  18.2 1.8 copy-start.2
  52.9 2.1 copy-start.6
  52.9 2.1 copy-start.18
  59.8 16.5 %copy-start.3 = (bf16[2,3,180,256]{3,0,2,1:T(2,128)(2,1)S(1)}, bf16[2,3,180,256]{3,0,2,1:T(2,128)(2,1)}, u32[]{:S(2)}) copy-start(bf16[2,3,180,256]{3,0,2,1:T(2,128)(2,1)} %param.8) | copy-start | bytes 1658884
  59.8 16.5 %copy-start.16 = (bf16[2,180,96]{2,1,0:T(8,128)(2,1)S(1)}, bf16[2,180,96]{2,1,0:T(8,128)(2,1)}, u32[]{:S(2)}) copy-start(bf16[2,180,96]{2,1,0:T(8,128)(2,1)} %pad_maximum_fusion.3) | copy-start | bytes 207364
  77.6 74.2 %reduce-scatter.5.cloned.1.call-start = ((), (), s32[]{:S(2)}) async-start(), calls=%async_computation.9 | async-start | bytes 2826240 | tf_op jit(solution)/shard_map/reduce_scatter | solution.py:194
  107.6 2.6 %copy-start.8 = (bf16[2,3,180,1024]{3,2,1,0:T(8,128)(2,1)S(1)}, bf16[2,3,180,1024]{3,2,1,0:T(8,128)(2,1)}, u32[]{:S(2)}) copy-start(bf16[2,3,180,1024]{3,2,1,0:T(8,128)(2,1)} %all-gather.5.cloned.1.call-done) | copy-start | bytes 6635524
  107.6 5.4 %slice-start = ((s8[4521984]{0:T(1024)(128)(4,1)}), s8[4194304]{0:T(1024)(128)(4,1)S(1)}, s32[]{:S(2)}) async-start(s8[4521984]{0:T(1024)(128)(4,1)} %bitcast.300), calls=%async_computation.10 | async-start | bytes 8388608
  110.2 2.9 %slice-start.1 = ((s8[4521984]{0:T(1024)(128)(4,1)}), s8[327680]{0:T(1024)(128)(4,1)S(1)}, s32[]{:S(2)}) async-start(s8[4521984]{0:T(1024)(128)(4,1)} %bitcast.300), calls=%async_computation.11 | async-start | bytes 655360
  113.0 5.4 %copy-start.19 = (f32[2,3,180,1024]{3,2,1,0:T(8,128)}, f32[2,3,180,1024]{3,2,1,0:T(8,128)S(1)}, u32[]{:S(2)}) copy-start(f32[2,3,180,1024]{3,2,1,0:T(8,128)S(1)} %fusion.14) | copy-start | bytes 13271044
  118.5 88.8 %reduce-scatter.3.cloned.1.call-start = ((), (), s32[]{:S(2)}) async-start(), calls=%async_computation.8 | async-start | bytes 2826240 | tf_op jit(solution)/shard_map/reduce_scatter | solution.py:194
  125.5 5.2 %collective-permute-start.4 = (f32[2,2,3,180]{3,2,1,0:T(4,128)S(1)}, f32[2,2,3,180]{3,2,1,0:T(4,128)S(1)}, u32[]{:S(2)}, u32[]{:S(2)}) collective-permute-start(f32[2,2,3,180]{3,2,1,0:T(4,128)S(1)} %pad_maximum_fusion.9), channel_id=1, source_target_pairs={{0,2},{1,3},{2,0},{3,1},{4,6},{5,7},{6,4},{7,5},{8,10},{9,11},{10,... | collective-permute-start | bytes 25928 | tf_op jit(solution)/shard_map/ppermute | solution.py:163
  128.0 4.0 %collective-permute-start.5 = (f32[2,2,3,180]{3,2,1,0:T(4,128)S(1)}, f32[2,2,3,180]{3,2,1,0:T(4,128)S(1)}, u32[]{:S(2)}, u32[]{:S(2)}) collective-permute-start(f32[2,2,3,180]{3,2,1,0:T(4,128)S(1)} %pad_maximum_fusion.9), channel_id=1, source_target_pairs={{0,1},{1,2},{2,3},{3,0},{4,5},{5,6},{6,7},{7,4},{8,9},{9,10},{10,1... | collective-permute-start | bytes 25928 | tf_op jit(solution)/shard_map/ppermute | solution.py:163
  128.0 4.0 %collective-permute-start.3 = (f32[2,2,3,180]{3,2,1,0:T(4,128)S(1)}, f32[2,2,3,180]{3,2,1,0:T(4,128)S(1)}, u32[]{:S(2)}, u32[]{:S(2)}) collective-permute-start(f32[2,2,3,180]{3,2,1,0:T(4,128)S(1)} %pad_maximum_fusion.9), channel_id=1, source_target_pairs={{0,3},{1,0},{2,1},{3,2},{4,7},{5,4},{6,5},{7,6},{8,11},{9,8},{10,9... | collective-permute-start | bytes 25928 | tf_op jit(solution)/shard_map/ppermute | solution.py:163
  178.5 2.1 copy-start.5
  182.3 17.0 %copy-start.13 = (bf16[2,3,180,256]{3,2,1,0:T(8,128)(2,1)S(1)}, bf16[2,3,180,256]{3,2,1,0:T(8,128)(2,1)}, u32[]{:S(2)}) copy-start(bf16[2,3,180,256]{3,2,1,0:T(8,128)(2,1)} %reduce-scatter.5.cloned.1.call-done) | copy-start | bytes 1658884
  183.0 16.4 %copy-start.4 = (bf16[2,3,180,256]{3,0,2,1:T(2,128)(2,1)S(1)}, bf16[2,3,180,256]{3,0,2,1:T(2,128)(2,1)}, u32[]{:S(2)}) copy-start(bf16[2,3,180,256]{3,0,2,1:T(2,128)(2,1)} %param.8) | copy-start | bytes 1658884
  183.0 16.4 %copy-start.7 = (bf16[2,3,180,256]{3,2,1,0:T(8,128)(2,1)S(1)}, bf16[2,3,180,256]{3,2,1,0:T(8,128)(2,1)}, u32[]{:S(2)}) copy-start(bf16[2,3,180,256]{3,2,1,0:T(8,128)(2,1)} %fusion.37) | copy-start | bytes 1658884
  183.0 16.4 %copy-start.9 = (bf16[2,3,180,256]{3,0,2,1:T(2,128)(2,1)S(1)}, bf16[2,3,180,256]{3,0,2,1:T(2,128)(2,1)}, u32[]{:S(2)}) copy-start(bf16[2,3,180,256]{3,0,2,1:T(2,128)(2,1)} %param.9) | copy-start | bytes 1658884
  183.0 16.4 %copy-start.12 = (f32[2,180,96]{2,1,0:T(8,128)S(1)}, f32[2,180,96]{2,1,0:T(8,128)}, u32[]{:S(2)}) copy-start(f32[2,180,96]{2,1,0:T(8,128)} %copy-done.11) | copy-start | bytes 414724
  202.1 4.2 %collective-permute-start.7 = (f32[2,2,3,180]{3,2,1,0:T(4,128)S(1)}, f32[2,2,3,180]{3,2,1,0:T(4,128)S(1)}, u32[]{:S(2)}, u32[]{:S(2)}) collective-permute-start(f32[2,2,3,180]{3,2,1,0:T(4,128)S(1)} %pad_maximum_fusion.10), channel_id=1, source_target_pairs={{0,2},{1,3},{2,0},{3,1},{4,6},{5,7},{6,4},{7,5},{8,10},{9,11},{10,... | collective-permute-start | bytes 25928 | tf_op jit(solution)/shard_map/ppermute | solution.py:163
  203.4 3.8 %collective-permute-start.8 = (f32[2,2,3,180]{3,2,1,0:T(4,128)S(1)}, f32[2,2,3,180]{3,2,1,0:T(4,128)S(1)}, u32[]{:S(2)}, u32[]{:S(2)}) collective-permute-start(f32[2,2,3,180]{3,2,1,0:T(4,128)S(1)} %pad_maximum_fusion.10), channel_id=1, source_target_pairs={{0,1},{1,2},{2,3},{3,0},{4,5},{5,6},{6,7},{7,4},{8,9},{9,10},{10,1... | collective-permute-start | bytes 25928 | tf_op jit(solution)/shard_map/ppermute | solution.py:163
  203.4 3.8 %collective-permute-start.6 = (f32[2,2,3,180]{3,2,1,0:T(4,128)S(1)}, f32[2,2,3,180]{3,2,1,0:T(4,128)S(1)}, u32[]{:S(2)}, u32[]{:S(2)}) collective-permute-start(f32[2,2,3,180]{3,2,1,0:T(4,128)S(1)} %pad_maximum_fusion.10), channel_id=1, source_target_pairs={{0,3},{1,0},{2,1},{3,2},{4,7},{5,4},{6,5},{7,6},{8,11},{9,8},{10,9... | collective-permute-start | bytes 25928 | tf_op jit(solution)/shard_map/ppermute | solution.py:163
  (3 other events, 3.7 us)
Sparse Core Ops, SparseCore 0:
  15.6 35.1 all-gather.2
  77.7 29.8 all-gather.4
  118.6 33.1 reduce-scatter.4
  154.2 30.7 reduce-scatter.2
where the time goes:
time: 220 us
  blocking collectives  79.8 us (36%)
  waiting for transfers between devices  45.3 us (21%)
  matrix products  38.3 us (17%)
  starting transfers between devices  15.8 us (7%)
  between operations  14.4 us (7%)
  local copies, waits for them, and re-layouts  13.1 us (6%)
  other arithmetic  12.9 us (6%)
    all_to_all x2, blocking collectives, stacked_columns(): lax.all_to_all(field.astype(link_type), 'space', 3, 2, tiled=True)  47.9 us
    all_to_all x2, blocking collectives, stacked_rows(): lax.all_to_all(field.astype(link_type), 'space', 2, 3, tiled=True)  31.9 us
    all_gather x1, waiting for transfers between devices, per_device(): whole_residual = lax.all_gather(residual, 'feat', axis=3, tiled=True)  23 us
    reduce_scatter x2, waiting for transfers between devices, channel_share(): lax.psum_scatter(term.astype(jnp.bfloat16), 'feat', scatter_dimension=3,...  19.8 us
    ppermute x9, starting transfers between devices, token_sums(): lax.ppermute(pair, 'feat', [(i, (i + count - shift) % count) for i in ran...  15.6 us
    dot_general x1, matrix products, per_device(): jnp.einsum('brwd,hd->brwh', whole_cotangent, down_weight, preferred_eleme...  6.92 us
    dot_general x1, matrix products, per_device(): jnp.einsum('brwh,hd->brwd', activated, down_weight, preferred_element_typ...  6.91 us
    dot_general x1, matrix products, per_device(): jnp.einsum('brwh,dh->brwd', grad_hidden, up_weight, preferred_element_typ...  5.41 us
  transfers between devices with their start and end apart: 13, of which 5 were waited for; matrix products, arithmetic and copies ran while one was open for 19% of the time, Pallas kernels for 0%

commit v1 on v0

--- a/solution.py
+++ b/solution.py
@@ -151,7 +151,15 @@
 
 
 def stacked_rows(field, link_type):
-    return lax.all_to_all(field.astype(link_type), "space", 2, 3, tiled=True).astype(jnp.float32)
+    return jnp.concatenate(
+        lax.all_to_all(
+            jnp.stack(jnp.split(field.astype(link_type), lax.psum(1, axis_name="space"), 2)),
+            axis_name="space",
+            split_axis=0,
+            concat_axis=0,
+        ),
+        3,
+    ).astype(jnp.float32)
 
 
 def token_sums(first_term, second_term):

time: 220 us -> 224 us (1.018)
  blocking collectives: 79.8 us -> 59.9 us
  waiting for transfers between devices: 45.3 us -> 57.2 us
  starting transfers between devices: 15.8 us -> 23.6 us
  local copies, waits for them, and re-layouts: 13.1 us -> 16.4 us
    all_to_all x2 -> x1, blocking collectives: 47.9 us -> 28.2 us  [stacked_columns(): lax.all_to_all(field.astype(link_type), 'space', 3, 2, tiled=True)]
    all_to_all x0 -> x1, starting transfers between devices: none -> 7.66 us  [stacked_columns(): lax.all_to_all(field.astype(link_type), 'space', 3, 2, tiled=True)]
    reduce_scatter x2, waiting for transfers between devices: 19.8 us -> 26.6 us  [channel_share(): lax.psum_scatter(term.astype(jnp.bfloat16), 'feat', scatter_dimension=3,...]
    all_to_all x0 -> x1, waiting for transfers between devices: none -> 5.13 us  [stacked_columns(): lax.all_to_all(field.astype(link_type), 'space', 3, 2, tiled=True)]
    unnamed x46 -> x108, local copies, waits for them, and re-layouts: 3.58 us -> 5.02 us
  transfers between devices with their start and end apart: 13 -> 14, of which waited for: 5 -> 6; matrix products, arithmetic and copies ran while one was open for 19% -> 18% of each run, Pallas kernels for 0% -> 0%
where the time goes in v1:
time: 224 us; the launch traced here: 223 us
  blocking collectives  59.9 us (27%)
  waiting for transfers between devices  57.2 us (26%)
  matrix products  38.3 us (17%)
  starting transfers between devices  23.6 us (11%)
  local copies, waits for them, and re-layouts  16.4 us (7%)
  between operations  14.7 us (7%)
  other arithmetic  12.9 us (6%)
    all_to_all x2, blocking collectives, stacked_rows(): lax.all_to_all(jnp.stack(jnp.split(field.astype(link_type), lax.psum(1, a...  31.8 us
    all_to_all x1, blocking collectives, stacked_columns(): lax.all_to_all(field.astype(link_type), 'space', 3, 2, tiled=True)  28.2 us
    reduce_scatter x2, waiting for transfers between devices, channel_share(): lax.psum_scatter(term.astype(jnp.bfloat16), 'feat', scatter_dimension=3,...  26.6 us
    all_gather x1, waiting for transfers between devices, per_device(): whole_residual = lax.all_gather(residual, 'feat', axis=3, tiled=True)  23.1 us
    ppermute x9, starting transfers between devices, token_sums(): lax.ppermute(pair, 'feat', [(i, (i + count - shift) % count) for i in ran...  15.6 us
    all_to_all x1, starting transfers between devices, stacked_columns(): lax.all_to_all(field.astype(link_type), 'space', 3, 2, tiled=True)  7.66 us
    dot_general x1, matrix products, per_device(): jnp.einsum('brwh,hd->brwd', activated, down_weight, preferred_element_typ...  6.91 us
    dot_general x1, matrix products, per_device(): jnp.einsum('brwd,hd->brwh', whole_cotangent, down_weight, preferred_eleme...  6.91 us
  transfers between devices with their start and end apart: 14, of which 6 were waited for; matrix products, arithmetic and copies ran while one was open for 18% of the time, Pallas kernels for 0%

profile of v1, /device:TPU:1, one launch (start us, length us, event | category | flops | bytes accessed | tf_op | source)
XLA Modules:
  0.0 223.2 jit_solution(12978386506528940776)
XLA Ops:
  7.2 1.7 convert_reduce_fusion.1
  9.0 3.8 %collective-permute-start.1 = (f32[2,2,3,180]{3,2,1,0:T(4,128)S(1)}, f32[2,2,3,180]{3,2,1,0:T(4,128)S(1)}, u32[]{:S(2)}, u32[]{:S(2)}) collective-permute-start(f32[2,2,3,180]{3,2,1,0:T(4,128)S(1)} %pad_maximum_fusion.8), channel_id=1, source_target_pairs={{0,2},{1,3},{2,0},{3,1},{4,6},{5,7},{6,4},{7,5},{8,10},{9,11},{10,... | collective-permute-start | bytes 25928 | tf_op jit(solution)/shard_map/ppermute | solution.py:171
  13.2 2.3 %collective-permute-start = (f32[2,2,3,180]{3,2,1,0:T(4,128)S(1)}, f32[2,2,3,180]{3,2,1,0:T(4,128)S(1)}, u32[]{:S(2)}, u32[]{:S(2)}) collective-permute-start(f32[2,2,3,180]{3,2,1,0:T(4,128)S(1)} %pad_maximum_fusion.8), channel_id=1, source_target_pairs={{0,3},{1,0},{2,1},{3,2},{4,7},{5,4},{6,5},{7,6},{8,11},{9,8},{10,9... | collective-permute-start | bytes 25928 | tf_op jit(solution)/shard_map/ppermute | solution.py:171
  22.0 28.2 %all_to_all.46 = f32[2,2,3,96,256]{4,1,2,0,3:T(2,128)S(1)} all-to-all(f32[2,2,3,96,256]{4,1,2,0,3:T(2,128)S(1)} %copy.90), channel_id=1, replica_groups=mesh['space'=32,'feat'=4] {'space'}, dimensions={3} | all-to-all | bytes 2359296 | tf_op jit(solution)/shard_map/all_to_all | solution.py:150
  51.3 1.6 reshape.207
  52.9 2.1 fusion.31
  57.7 1.4 fusion.42
  60.6 16.0 %all_to_all.47 = bf16[32,2,2,3,3,256]{5,2,4,3,1,0:T(2,128)(2,1)S(1)} all-to-all(bf16[32,2,2,3,3,256]{5,2,4,3,1,0:T(2,128)(2,1)S(1)} %copy.102), channel_id=1, replica_groups=mesh['space'=32,'feat'=4] {'space'}, dimensions={0} | all-to-all | bytes 1179648 | tf_op jit(solution)/shard_map/all_to_all | solution.py:155
  77.0 1.3 fusion.37
  78.4 6.9 %fusion.16 = f32[2,3,180,1024]{3,2,1,0:T(8,128)} fusion(bf16[2,3,180,1024]{3,0,2,1:T(2,128)(2,1)} %all-gather.3.cloned.1.call-done, bf16[1024,1024]{1,0:T(8,128)(2,1)} %param.15), kind=kOutput, calls=%fused_computation.20 | convolution fusion | flops 2264924160 | bytes 8732672 | tf_op jit(solution)/shard_map/brwd,hd->brwh/dot_general | solution.py:259
  85.3 23.1 %all-gather.5.cloned.1.call-done = bf16[2,3,180,1024]{3,2,1,0:T(8,128)(2,1)} async-done(((bf16[2,3,180,256]{3,2,1,0:T(8,128)(2,1)}), bf16[2,3,180,1024]{3,2,1,0:T(8,128)(2,1)}) %all-gather.5.cloned.1.call-update) | async-done | bytes 2211856 | tf_op jit(solution)/shard_map/all_gather | solution.py:258
  108.3 2.5 %convert_reduce_fusion = (f32[2,3,180]{2,1,0:T(4,128)S(1)}, f32[2,3,180]{2,1,0:T(4,128)S(1)}) fusion(bf16[2,3,180,1024]{3,2,1,0:T(8,128)(2,1)} %all-gather.5.cloned.1.call-done), kind=kLoop, calls=%fused_computation.3 | loop fusion | flops 4421520 | bytes 2220480 | tf_op jit(solution)/shard_map/reduce_sum | solution.py:264
  110.9 2.8 %fusion.14 = f32[2,3,180,1024]{3,2,1,0:T(8,128)S(1)} fusion(bf16[2,3,180,1024]{3,2,1,0:T(8,128)(2,1)S(1)} %copy-done.8, f32[2,3,180]{2,1,0:T(4,128)S(1)} %get-tuple-element.60, f32[2,3,180]{2,1,0:T(4,128)S(1)} %get-tuple-element.59, bf16[1024,1024]{1,0:T(8,128)(2,1)S(1)} %copy-done), kind=kOutput, calls=%fused_computation.19 | convolution fusion | flops 2269347840 | bytes 8741312 | tf_op jit(solution)/shard_map/brwd,dh->brwh/dot_general | solution.py:268
  113.8 5.4 %fusion.123 = (f32[2,3,180]{2,1,0:T(4,128)S(1)}, f32[2,3,180]{2,1,0:T(4,128)S(1)}, bf16[2,3,180,1024]{3,2,1,0:T(8,128)(2,1)}) fusion(f32[2,3,180]{2,1,0:T(4,128)S(1)} %get-tuple-element.60, f32[2,3,180]{2,1,0:T(4,128)S(1)} %get-tuple-element.59, bf16[2,3,180,1024]{3,2,1,0:T(8,128)(2,1)S(1)} %copy-done.8, bf16[1024,1024]{1,0:T(8,128)(2,1)S(1)} %copy-done, ...), kind=kOutput, calls=%fused_computation.317 | convolution fusion | flops 2283722752 | bytes 15385472 | tf_op jit(solution)/shard_map/brwh,dh->brwd/dot_general | solution.py:277
  119.3 2.5 %collective-permute-start.4 = (f32[2,2,3,180]{3,2,1,0:T(4,128)S(1)}, f32[2,2,3,180]{3,2,1,0:T(4,128)S(1)}, u32[]{:S(2)}, u32[]{:S(2)}) collective-permute-start(f32[2,2,3,180]{3,2,1,0:T(4,128)S(1)} %pad_maximum_fusion.9), channel_id=1, source_target_pairs={{0,2},{1,3},{2,0},{3,1},{4,6},{5,7},{6,4},{7,5},{8,10},{9,11},{10,... | collective-permute-start | bytes 25928 | tf_op jit(solution)/shard_map/ppermute | solution.py:171
  121.8 2.7 %collective-permute-start.3 = (f32[2,2,3,180]{3,2,1,0:T(4,128)S(1)}, f32[2,2,3,180]{3,2,1,0:T(4,128)S(1)}, u32[]{:S(2)}, u32[]{:S(2)}) collective-permute-start(f32[2,2,3,180]{3,2,1,0:T(4,128)S(1)} %pad_maximum_fusion.9), channel_id=1, source_target_pairs={{0,3},{1,0},{2,1},{3,2},{4,7},{5,4},{6,5},{7,6},{8,11},{9,8},{10,9... | collective-permute-start | bytes 25928 | tf_op jit(solution)/shard_map/ppermute | solution.py:171
  124.5 1.3 collective-permute-done.5
  125.8 26.6 %reduce-scatter.5.cloned.1.call-done = bf16[2,3,180,256]{3,2,1,0:T(8,128)(2,1)} async-done(((bf16[2,3,180,1024]{3,2,1,0:T(8,128)(2,1)}), bf16[2,3,180,256]{3,2,1,0:T(8,128)(2,1)}) %reduce-scatter.5.cloned.1.call-update) | async-done | bytes 552976 | tf_op jit(solution)/shard_map/reduce_scatter | solution.py:202
  152.3 2.3 %fusion.40 = bf16[2,2,3,96,256]{4,3,2,1,0:T(8,128)(2,1)S(1)} fusion(bf16[2,180,96]{2,1,0:T(8,128)(2,1)} %pad_maximum_fusion.3, bf16[2,3,180,256]{3,2,1,0:T(8,128)(2,1)} %fusion.37, bf16[2,3,180,256]{3,2,1,0:T(8,128)(2,1)} %reduce-scatter.5.cloned.1.call-done, bf16[2,3,180,256]{3,0,2,1:T(2,128)(2,1)} %param.9, f32[2,3,180]{2,1,0:T(4,128)S(1)} %get-tuple-element.58, ...), kind=kOutput, calls=%fused_computation.61 | convolution fusion | flops 108933120 | bytes 2335104 | tf_op jit(solution)/shard_map/brwc,pwk->pbrkc/dot_general | solution.py:130
  154.7 1.5 copy.107
  156.2 7.7 %all-to-all-start.2 = ((bf16[2,2,3,96,256]{4,1,2,0,3:T(2,128)(2,1)}), bf16[2,2,3,96,256]{4,1,2,0,3:T(2,128)(2,1)}, u32[]{:S(2)}, u32[]{:S(2)}) async-start(bf16[2,2,3,96,256]{4,1,2,0,3:T(2,128)(2,1)} %copy.107), calls=%async_computation.4 | async-start | bytes 1179648 | tf_op jit(solution)/shard_map/all_to_all | solution.py:150
  164.1 6.9 %fusion.28 = bf16[2,3,180,1024]{3,2,1,0:T(8,128)(2,1)} fusion(bf16[1024,1024]{1,0:T(8,128)(2,1)} %param.15, f32[2,3,180,1024]{3,2,1,0:T(8,128)} %copy-done.19), kind=kOutput, calls=%fused_computation.36 | convolution fusion | flops 2271559680 | bytes 8732672 | tf_op jit(solution)/shard_map/brwh,hd->brwd/dot_general | solution.py:272
  171.0 5.1 %all-to-all-done.2 = bf16[2,2,3,96,256]{4,1,2,0,3:T(2,128)(2,1)} async-done(((bf16[2,2,3,96,256]{4,1,2,0,3:T(2,128)(2,1)}), bf16[2,2,3,96,256]{4,1,2,0,3:T(2,128)(2,1)}, u32[]{:S(2)}, u32[]{:S(2)}) %all-to-all-start.2) | async-done | bytes 589856 | tf_op jit(solution)/shard_map/all_to_all | solution.py:150
  176.2 1.5 copy.109
  177.6 1.2 convolution_bitcast_fusion.8
  178.9 2.6 %reshape.245 = bf16[2,2,96,3,2,128]{5,4,2,0,3,1:T(2,128)(2,1)} reshape(bf16[2,2,96,3,256]{4,2,0,3,1:T(8,128)(2,1)} %convolution_bitcast_fusion.8) | data formatting | bytes 1179648 | tf_op jit(solution)/shard_map/reshape | solution.py:60
  181.5 2.1 fusion.39
  186.7 15.8 %all_to_all.48 = bf16[32,2,2,3,3,256]{5,2,4,3,1,0:T(2,128)(2,1)S(1)} all-to-all(bf16[32,2,2,3,3,256]{5,2,4,3,1,0:T(2,128)(2,1)S(1)} %copy.119), channel_id=1, replica_groups=mesh['space'=32,'feat'=4] {'space'}, dimensions={0} | all-to-all | bytes 1179648 | tf_op jit(solution)/shard_map/all_to_all | solution.py:155
  203.0 2.7 %fusion.124 = (f32[2,3,180]{2,1,0:T(4,128)S(1)}, f32[2,3,180]{2,1,0:T(4,128)S(1)}, f32[2,3,180,256]{3,2,1,0:T(8,128)}) fusion(f32[2,3,180]{2,1,0:T(4,128)S(1)} %fusion.115, f32[2,3,180]{2,1,0:T(4,128)S(1)} %fusion.116, bf16[2,3,180,256]{3,0,2,1:T(2,128)(2,1)S(1)} %copy-done.4, bf16[2,2,3,96,256]{4,1,3,2,0:T(2,128)(2,1)S(1)} %bitcast.535, ...), kind=kOutput, calls=%fused_computation.318 | convolution fusion | flops 110866320 | bytes 4080384 | tf_op jit(solution)/shard_map/pbrkc,pwk->brwc/dot_general | solution.py:134
  206.9 2.7 %collective-permute-start.6 = (f32[2,2,3,180]{3,2,1,0:T(4,128)S(1)}, f32[2,2,3,180]{3,2,1,0:T(4,128)S(1)}, u32[]{:S(2)}, u32[]{:S(2)}) collective-permute-start(f32[2,2,3,180]{3,2,1,0:T(4,128)S(1)} %pad_maximum_fusion.10), channel_id=1, source_target_pairs={{0,3},{1,0},{2,1},{3,2},{4,7},{5,4},{6,5},{7,6},{8,11},{9,8},{10,9... | collective-permute-start | bytes 25928 | tf_op jit(solution)/shard_map/ppermute | solution.py:171
  210.8 3.4 %fusion.68 = (bf16[2,3,180,256]{3,2,1,0:T(8,128)(2,1)S(1)}, bf16[2,3,180,256]{3,2,1,0:T(8,128)(2,1)S(1)}) fusion(f32[2,3,180,256]{3,2,1,0:T(8,128)} %get-tuple-element.64, f32[2,3,180]{2,1,0:T(4,128)S(1)} %get-tuple-element.56, f32[2,3,180]{2,1,0:T(4,128)S(1)} %get-tuple-element.55, f32[2,3,180]{2,1,0:T(4,128)S(1)} %fusion.115, ...), kind=kLoop, calls=%fused_computation.92 | loop fusion | flops 6082560 | bytes 5011200 | tf_op jit(solution)/shard_map/convert_element_type | solution.py:313
  214.2 1.2 copy.123
  (176 shorter events, 19.6 us)
Async XLA Ops:
  7.2 103.7 %copy-start = (bf16[1024,1024]{1,0:T(8,128)(2,1)S(1)}, bf16[1024,1024]{1,0:T(8,128)(2,1)}, u32[]{:S(2)}) copy-start(bf16[1024,1024]{1,0:T(8,128)(2,1)} %param.14) | copy-start | bytes 6291460
  7.2 10.1 %copy-start.14 = (f32[2,2,128,128]{3,2,1,0:T(8,128)S(1)}, f32[2,2,128,128]{3,2,1,0:T(8,128)}, u32[]{:S(2)}) copy-start(f32[2,2,128,128]{3,2,1,0:T(8,128)} %param.10) | copy-start | bytes 786436
  7.2 50.5 %all-gather.3.cloned.1.call-start = ((), (), s32[]{:S(2)}) async-start(), calls=%async_computation.6 | async-start | bytes 2764800 | tf_op jit(solution)/shard_map/all_gather | solution.py:235
  9.0 8.4 %copy-start.15 = (f32[2,2,128,128]{3,2,1,0:T(8,128)S(1)}, f32[2,2,128,128]{3,2,1,0:T(8,128)}, u32[]{:S(2)}) copy-start(f32[2,2,128,128]{3,2,1,0:T(8,128)} %param.12) | copy-start | bytes 786436
  9.0 11.0 %collective-permute-start.1 = (f32[2,2,3,180]{3,2,1,0:T(4,128)S(1)}, f32[2,2,3,180]{3,2,1,0:T(4,128)S(1)}, u32[]{:S(2)}, u32[]{:S(2)}) collective-permute-start(f32[2,2,3,180]{3,2,1,0:T(4,128)S(1)} %pad_maximum_fusion.8), channel_id=1, source_target_pairs={{0,2},{1,3},{2,0},{3,1},{4,6},{5,7},{6,4},{7,5},{8,10},{9,11},{10,... | collective-permute-start | bytes 25928 | tf_op jit(solution)/shard_map/ppermute | solution.py:171
  12.8 7.2 %collective-permute-start.2 = (f32[2,2,3,180]{3,2,1,0:T(4,128)S(1)}, f32[2,2,3,180]{3,2,1,0:T(4,128)S(1)}, u32[]{:S(2)}, u32[]{:S(2)}) collective-permute-start(f32[2,2,3,180]{3,2,1,0:T(4,128)S(1)} %pad_maximum_fusion.8), channel_id=1, source_target_pairs={{0,1},{1,2},{2,3},{3,0},{4,5},{5,6},{6,7},{7,4},{8,9},{9,10},{10,1... | collective-permute-start | bytes 25928 | tf_op jit(solution)/shard_map/ppermute | solution.py:171
  13.2 6.8 %collective-permute-start = (f32[2,2,3,180]{3,2,1,0:T(4,128)S(1)}, f32[2,2,3,180]{3,2,1,0:T(4,128)S(1)}, u32[]{:S(2)}, u32[]{:S(2)}) collective-permute-start(f32[2,2,3,180]{3,2,1,0:T(4,128)S(1)} %pad_maximum_fusion.8), channel_id=1, source_target_pairs={{0,3},{1,0},{2,1},{3,2},{4,7},{5,4},{6,5},{7,6},{8,11},{9,8},{10,9... | collective-permute-start | bytes 25928 | tf_op jit(solution)/shard_map/ppermute | solution.py:171
  15.5 92.8 %all-gather.5.cloned.1.call-start = ((), (), s32[]{:S(2)}) async-start(), calls=%async_computation.7 | async-start | bytes 2826240 | tf_op jit(solution)/shard_map/all_gather | solution.py:258
  17.4 2.7 %copy-start.11 = (f32[2,180,96]{2,1,0:T(8,128)}, f32[2,180,96]{2,1,0:T(8,128)S(1)}, u32[]{:S(2)}) copy-start(f32[2,180,96]{2,1,0:T(8,128)S(1)} %pad_maximum_fusion.2) | copy-start | bytes 414724
  52.9 2.1 copy-start.6
  52.9 2.1 copy-start.18
  60.5 16.4 %copy-start.3 = (bf16[2,3,180,256]{3,0,2,1:T(2,128)(2,1)S(1)}, bf16[2,3,180,256]{3,0,2,1:T(2,128)(2,1)}, u32[]{:S(2)}) copy-start(bf16[2,3,180,256]{3,0,2,1:T(2,128)(2,1)} %param.8) | copy-start | bytes 1658884
  60.6 16.4 %copy-start.16 = (bf16[2,180,96]{2,1,0:T(8,128)(2,1)S(1)}, bf16[2,180,96]{2,1,0:T(8,128)(2,1)}, u32[]{:S(2)}) copy-start(bf16[2,180,96]{2,1,0:T(8,128)(2,1)} %pad_maximum_fusion.3) | copy-start | bytes 207364
  78.3 74.0 %reduce-scatter.5.cloned.1.call-start = ((), (), s32[]{:S(2)}) async-start(), calls=%async_computation.9 | async-start | bytes 2826240 | tf_op jit(solution)/shard_map/reduce_scatter | solution.py:202
  108.3 2.6 %copy-start.8 = (bf16[2,3,180,1024]{3,2,1,0:T(8,128)(2,1)S(1)}, bf16[2,3,180,1024]{3,2,1,0:T(8,128)(2,1)}, u32[]{:S(2)}) copy-start(bf16[2,3,180,1024]{3,2,1,0:T(8,128)(2,1)} %all-gather.5.cloned.1.call-done) | copy-start | bytes 6635524
  108.3 5.4 %slice-start = ((s8[4521984]{0:T(1024)(128)(4,1)}), s8[4194304]{0:T(1024)(128)(4,1)S(1)}, s32[]{:S(2)}) async-start(s8[4521984]{0:T(1024)(128)(4,1)} %bitcast.551), calls=%async_computation.10 | async-start | bytes 8388608
  110.9 2.9 %slice-start.1 = ((s8[4521984]{0:T(1024)(128)(4,1)}), s8[327680]{0:T(1024)(128)(4,1)S(1)}, s32[]{:S(2)}) async-start(s8[4521984]{0:T(1024)(128)(4,1)} %bitcast.551), calls=%async_computation.11 | async-start | bytes 655360
  113.8 5.4 %copy-start.19 = (f32[2,3,180,1024]{3,2,1,0:T(8,128)}, f32[2,3,180,1024]{3,2,1,0:T(8,128)S(1)}, u32[]{:S(2)}) copy-start(f32[2,3,180,1024]{3,2,1,0:T(8,128)S(1)} %fusion.14) | copy-start | bytes 13271044
  119.3 5.2 %collective-permute-start.4 = (f32[2,2,3,180]{3,2,1,0:T(4,128)S(1)}, f32[2,2,3,180]{3,2,1,0:T(4,128)S(1)}, u32[]{:S(2)}, u32[]{:S(2)}) collective-permute-start(f32[2,2,3,180]{3,2,1,0:T(4,128)S(1)} %pad_maximum_fusion.9), channel_id=1, source_target_pairs={{0,2},{1,3},{2,0},{3,1},{4,6},{5,7},{6,4},{7,5},{8,10},{9,11},{10,... | collective-permute-start | bytes 25928 | tf_op jit(solution)/shard_map/ppermute | solution.py:171
  121.8 3.9 %collective-permute-start.5 = (f32[2,2,3,180]{3,2,1,0:T(4,128)S(1)}, f32[2,2,3,180]{3,2,1,0:T(4,128)S(1)}, u32[]{:S(2)}, u32[]{:S(2)}) collective-permute-start(f32[2,2,3,180]{3,2,1,0:T(4,128)S(1)} %pad_maximum_fusion.9), channel_id=1, source_target_pairs={{0,1},{1,2},{2,3},{3,0},{4,5},{5,6},{6,7},{7,4},{8,9},{9,10},{10,1... | collective-permute-start | bytes 25928 | tf_op jit(solution)/shard_map/ppermute | solution.py:171
  121.8 3.9 %collective-permute-start.3 = (f32[2,2,3,180]{3,2,1,0:T(4,128)S(1)}, f32[2,2,3,180]{3,2,1,0:T(4,128)S(1)}, u32[]{:S(2)}, u32[]{:S(2)}) collective-permute-start(f32[2,2,3,180]{3,2,1,0:T(4,128)S(1)} %pad_maximum_fusion.9), channel_id=1, source_target_pairs={{0,3},{1,0},{2,1},{3,2},{4,7},{5,4},{6,5},{7,6},{8,11},{9,8},{10,9... | collective-permute-start | bytes 25928 | tf_op jit(solution)/shard_map/ppermute | solution.py:171
  156.2 20.0 %all-to-all-start.2 = ((bf16[2,2,3,96,256]{4,1,2,0,3:T(2,128)(2,1)}), bf16[2,2,3,96,256]{4,1,2,0,3:T(2,128)(2,1)}, u32[]{:S(2)}, u32[]{:S(2)}) async-start(bf16[2,2,3,96,256]{4,1,2,0,3:T(2,128)(2,1)} %copy.107), calls=%async_computation.4 | async-start | bytes 1179648 | tf_op jit(solution)/shard_map/all_to_all | solution.py:150
  163.8 47.0 %reduce-scatter.3.cloned.1.call-start = ((), (), s32[]{:S(2)}) async-start(), calls=%async_computation.8 | async-start | bytes 2826240 | tf_op jit(solution)/shard_map/reduce_scatter | solution.py:202
  181.4 2.1 copy-start.5
  186.2 16.8 %copy-start.13 = (bf16[2,3,180,256]{3,2,1,0:T(8,128)(2,1)S(1)}, bf16[2,3,180,256]{3,2,1,0:T(8,128)(2,1)}, u32[]{:S(2)}) copy-start(bf16[2,3,180,256]{3,2,1,0:T(8,128)(2,1)} %reduce-scatter.5.cloned.1.call-done) | copy-start | bytes 1658884
  186.7 16.2 %copy-start.4 = (bf16[2,3,180,256]{3,0,2,1:T(2,128)(2,1)S(1)}, bf16[2,3,180,256]{3,0,2,1:T(2,128)(2,1)}, u32[]{:S(2)}) copy-start(bf16[2,3,180,256]{3,0,2,1:T(2,128)(2,1)} %param.8) | copy-start | bytes 1658884
  186.7 16.2 %copy-start.7 = (bf16[2,3,180,256]{3,2,1,0:T(8,128)(2,1)S(1)}, bf16[2,3,180,256]{3,2,1,0:T(8,128)(2,1)}, u32[]{:S(2)}) copy-start(bf16[2,3,180,256]{3,2,1,0:T(8,128)(2,1)} %fusion.37) | copy-start | bytes 1658884
  186.7 16.2 %copy-start.9 = (bf16[2,3,180,256]{3,0,2,1:T(2,128)(2,1)S(1)}, bf16[2,3,180,256]{3,0,2,1:T(2,128)(2,1)}, u32[]{:S(2)}) copy-start(bf16[2,3,180,256]{3,0,2,1:T(2,128)(2,1)} %param.9) | copy-start | bytes 1658884
  186.7 16.2 %copy-start.12 = (f32[2,180,96]{2,1,0:T(8,128)S(1)}, f32[2,180,96]{2,1,0:T(8,128)}, u32[]{:S(2)}) copy-start(f32[2,180,96]{2,1,0:T(8,128)} %copy-done.11) | copy-start | bytes 414724
  205.7 4.2 %collective-permute-start.7 = (f32[2,2,3,180]{3,2,1,0:T(4,128)S(1)}, f32[2,2,3,180]{3,2,1,0:T(4,128)S(1)}, u32[]{:S(2)}, u32[]{:S(2)}) collective-permute-start(f32[2,2,3,180]{3,2,1,0:T(4,128)S(1)} %pad_maximum_fusion.10), channel_id=1, source_target_pairs={{0,2},{1,3},{2,0},{3,1},{4,6},{5,7},{6,4},{7,5},{8,10},{9,11},{10,... | collective-permute-start | bytes 25928 | tf_op jit(solution)/shard_map/ppermute | solution.py:171
  206.9 3.8 %collective-permute-start.8 = (f32[2,2,3,180]{3,2,1,0:T(4,128)S(1)}, f32[2,2,3,180]{3,2,1,0:T(4,128)S(1)}, u32[]{:S(2)}, u32[]{:S(2)}) collective-permute-start(f32[2,2,3,180]{3,2,1,0:T(4,128)S(1)} %pad_maximum_fusion.10), channel_id=1, source_target_pairs={{0,1},{1,2},{2,3},{3,0},{4,5},{5,6},{6,7},{7,4},{8,9},{9,10},{10,1... | collective-permute-start | bytes 25928 | tf_op jit(solution)/shard_map/ppermute | solution.py:171
  206.9 3.8 %collective-permute-start.6 = (f32[2,2,3,180]{3,2,1,0:T(4,128)S(1)}, f32[2,2,3,180]{3,2,1,0:T(4,128)S(1)}, u32[]{:S(2)}, u32[]{:S(2)}) collective-permute-start(f32[2,2,3,180]{3,2,1,0:T(4,128)S(1)} %pad_maximum_fusion.10), channel_id=1, source_target_pairs={{0,3},{1,0},{2,1},{3,2},{4,7},{5,4},{6,5},{7,6},{8,11},{9,8},{10,9... | collective-permute-start | bytes 25928 | tf_op jit(solution)/shard_map/ppermute | solution.py:171
  (4 other events, 5.5 us)
Sparse Core Ops, SparseCore 0:
  15.6 35.1 all-gather.2
  78.4 29.8 all-gather.4
  119.4 32.9 reduce-scatter.4
  171.1 30.4 reduce-scatter.2
